TPU v7x, 32 devices: a whole 2x2x4 slice. The times are simulated.
32 devices in a mesh: obs: 16 (over z, x, core), freq: 2 (over y).
Axes of the slice: x: 2, y: 2, z: 4, core: 2. Of those that a mesh axis runs over, the one named last changes fastest.
Arguments:
- cell_spectra: bfloat16 [8192, 512], P('obs', 'freq'), may hold values from -6 to 6
- cell_weight: float32 [8192], P('obs'), may hold values from 0.25 to 1
- cell_owner: int32 [8192, 1], P('obs'), may hold values from 0 to 15; in each aligned block of 512 rows (0 to 511, 512 to 1023, ...) at most 80 rows name the same one
- cell_local: int32 [8192], P('obs'), may hold values from 0 to 31
- panel_position: float32 [3, 512], replicated, may hold values from -8 to 8
- observer_position: float32 [3, 1024], P(None, 'obs'), may hold values from -40 to 40, as said below
Outputs:
- pressure: float32 [64, 2, 1024], P('freq', None, 'obs')
- level: float32 [1024], P('obs')
Inputs may be any that keep to these rules, and one draw needn't show every extreme that they name: `cell_owner`: among the 512 cells of one partition at most 80 name one panel group, and in every draw some partition sends exactly 80 cells to one group. `observer_position`: every observer lies between 20 and 40 from the anchor (0, 0, 0).
All inputs are finite; a program needn't handle non-finite values.
Results may differ from a plain program's by a relative error of at most 0.0029.
Values may be sent and summed in bfloat16 or wider, within the bound.
No kernel may reach another device: no remote copies, remote signals or barrier semaphores. Data moves between devices by JAX's collectives and lax.ppermute only.
A program may use at most 64 MiB of HBM per device.

v0:
```python
import math
import jax
import jax.numpy as jnp
from jax import lax
from jax.sharding import PartitionSpec as P

wave_step = 0.1
reference_radius = 10.0


def phase_powers(distance, wave_numbers):
    needed = wave_numbers.shape[0]
    cosine = jnp.cos(wave_numbers[0] * distance)[None]
    sine = jnp.sin(wave_numbers[0] * distance)[None]
    step_cos = jnp.cos(wave_step * distance)[None]
    step_sin = jnp.sin(wave_step * distance)[None]
    while cosine.shape[0] < needed:
        later_cos = cosine * step_cos - sine * step_sin
        later_sin = sine * step_cos + cosine * step_sin
        cosine = jnp.concatenate([cosine, later_cos], axis=0)
        sine = jnp.concatenate([sine, later_sin], axis=0)
        step_cos, step_sin = (step_cos * step_cos - step_sin * step_sin, 2.0 * step_cos * step_sin)
    return (cosine, sine)


def kernel_block(source, panel_points, observer_points, wave_numbers):
    offsets = observer_points[:, None, :] - panel_points[:, :, None]
    distance = jnp.sqrt(offsets[0] * offsets[0] + offsets[1] * offsets[1] + offsets[2] * offsets[2])
    inverse = 1.0 / distance
    heading = offsets * inverse[None]
    channels = jnp.transpose(source, (2, 1, 0))
    dipole_real = (
        heading[0][None] * channels[2][:, :, None]
        + heading[1][None] * channels[4][:, :, None]
        + heading[2][None] * channels[6][:, :, None]
    )
    dipole_imag = (
        heading[0][None] * channels[3][:, :, None]
        + heading[1][None] * channels[5][:, :, None]
        + heading[2][None] * channels[7][:, :, None]
    )
    waves = wave_numbers[:, None, None]
    amp_real = channels[0][:, :, None] + dipole_real * inverse[None] - waves * dipole_imag
    amp_imag = channels[1][:, :, None] + dipole_imag * inverse[None] + waves * dipole_real
    cosine, sine = phase_powers(distance, wave_numbers)
    weight_real = cosine * inverse[None]
    weight_imag = sine * inverse[None]
    real_part = jnp.sum(weight_real * amp_real + weight_imag * amp_imag, axis=1)
    imag_part = jnp.sum(weight_real * amp_imag - weight_imag * amp_real, axis=1)
    return jnp.stack([real_part, imag_part], axis=1)


def shards(cell_spectra, cell_weight, cell_owner, cell_local, panel_position, observer_position):
    cell_rows, columns = cell_spectra.shape
    freqs_dev = columns // 8
    groups = lax.axis_size("obs")
    panel_total = panel_position.shape[1]
    panels_dev = panel_total // groups
    observers_dev = observer_position.shape[1]
    weighted = (cell_weight[:, None] * cell_spectra.astype(jnp.float32)).astype(jnp.bfloat16)
    panel_index = cell_owner[:, 0] * panels_dev + cell_local
    selector = (jnp.arange(panel_total, dtype=jnp.int32)[:, None] == panel_index[None, :]).astype(
        jnp.bfloat16
    )
    local_source = jnp.dot(selector, weighted, preferred_element_type=jnp.float32)
    group_first = lax.axis_index("freq") * freqs_dev
    wave_numbers = wave_step * (
        (group_first + jnp.arange(freqs_dev, dtype=jnp.int32)).astype(jnp.float32) + 1.0
    )
    start_value = jnp.zeros((freqs_dev, 2, observers_dev), jnp.float32)
    arrived = lax.all_to_all(
        local_source.reshape(groups, panels_dev, columns), "obs", 0, 0, tiled=True
    )
    own_source = jnp.sum(arrived, axis=0)
    portion = lax.all_to_all(
        jnp.broadcast_to(own_source[None], (groups, panels_dev, columns)), "obs", 0, 0, tiled=True
    ).reshape(panel_total, columns)
    rows_count = portion.shape[0]
    tile_rows = math.gcd(rows_count, 256)

    def advance(turn, accum):
        source = lax.dynamic_slice_in_dim(portion, turn * tile_rows, tile_rows, 0).reshape(
            tile_rows, freqs_dev, 8
        )
        points = lax.dynamic_slice_in_dim(panel_position, turn * tile_rows, tile_rows, 1)
        return accum + kernel_block(source, points, observer_position, wave_numbers)

    summed = lax.fori_loop(0, rows_count // tile_rows, advance, start_value)
    pressure = summed * (reference_radius / math.sqrt(panel_total))
    energy = jnp.sum(pressure[:, 0] * pressure[:, 0] + pressure[:, 1] * pressure[:, 1], axis=0)
    if lax.axis_size("freq") == 2:
        band_total = energy + lax.ppermute(energy, "freq", [(0, 1), (1, 0)])
    else:
        band_total = lax.psum(energy, "freq")
    level = jnp.log(band_total / (freqs_dev * lax.axis_size("freq")) + 1e-06)
    return (pressure, level)


def solution(mesh):
    in_specs = (P("obs", "freq"), P("obs"), P("obs", None), P("obs"), P(), P(None, "obs"))
    out_specs = (P("freq", None, "obs"), P("obs"))
    return jax.shard_map(shards, mesh=mesh, in_specs=in_specs, out_specs=out_specs, check_vma=False)
```

profile of v0, /device:TPU:0, one launch (start us, length us, event | category | flops | bytes accessed | tf_op | source)
XLA Modules:
  0.0 64.2 jit_solution(14932165219836297983)
XLA Ops:
  0.6 0.0 copy-start.3
  0.6 0.0 copy-start.1
  0.7 0.7 %broadcast_multiply_fusion.1 = s32[512,1]{0,1:T(1,128)S(1)} fusion(s32[512,1]{0,1:T(1,128)} %param.10), kind=kLoop, calls=%fused_computation.92 | loop fusion | flops 512 | bytes 4096 | tf_op jit(solution)/shard_map/mul | solution.py:61
  1.3 0.7 %add.278 = s32[512]{0:T(512)S(1)} add(s32[512]{0:T(512)S(1)} %bitcast.81, s32[512]{0:T(512)} %param.11) | non-fusion elementwise | flops 512 | bytes 6144 | tf_op jit(solution)/shard_map/add | solution.py:61
  2.0 1.4 %fusion.12 = f32[512,256]{1,0:T(8,128)S(1)} fusion(s32[512]{0:T(512)S(1)} %add.278, bf16[512,256]{1,0:T(8,128)(2,1)} %param.8, f32[512]{0:T(512)} %param.9), kind=kOutput, calls=%fused_computation.83 | convolution fusion | flops 134873088 | bytes 790528 | tf_op jit(solution)/shard_map/dot_general | solution.py:65
  3.4 21.6 %all_to_all.10 = f32[16,32,256]{2,1,0:T(8,128)S(1)} all-to-all(f32[16,32,256]{2,1,0:T(8,128)S(1)} %bitcast.78), channel_id=1, replica_groups=mesh['obs'=16,'freq'=2] {'obs'}, dimensions={0} | all-to-all | bytes 1048576 | tf_op jit(solution)/shard_map/all_to_all | solution.py:71
  25.1 0.8 %broadcast_in_dim.41 = f32[16,32,256]{2,1,0:T(8,128)} broadcast(f32[32,256]{1,0:T(8,128)S(1)} %reduce_sum.44), dimensions={1,2} | broadcast | bytes 557056 | tf_op jit(solution)/shard_map/broadcast_in_dim | solution.py:76
  25.9 4.1 %all-to-all-start.1 = ((f32[16,32,256]{2,1,0:T(8,128)}), f32[16,32,256]{2,1,0:T(8,128)S(1)}, u32[]{:S(2)}, u32[]{:S(2)}) async-start(f32[16,32,256]{2,1,0:T(8,128)} %broadcast_in_dim.41), calls=%async_computation.1 | async-start | bytes 1048576 | tf_op jit(solution)/shard_map/all_to_all | solution.py:75
  30.0 14.4 %all-to-all-done.1 = f32[16,32,256]{2,1,0:T(8,128)S(1)} async-done(((f32[16,32,256]{2,1,0:T(8,128)}), f32[16,32,256]{2,1,0:T(8,128)S(1)}, u32[]{:S(2)}, u32[]{:S(2)}) %all-to-all-start.1) | async-done | bytes 524320 | tf_op jit(solution)/shard_map/all_to_all | solution.py:75
  44.5 0.0 copy-done.3
  44.5 0.0 copy-done.1
  44.5 15.4 %while.14 = (s32[]{:T(128)}, f32[32,2,64]{2,0,1:T(8,128)S(1)}, f32[32]{0:T(128)S(1)}, f32[3,64]{1,0:T(4,128)S(1)}, f32[3,512]{1,0:T(4,128)S(1)}, /*index=5*/f32[...) while((s32[]{:T(128)}, f32[32,2,64]{2,0,1:T(8,128)S(1)}, f32[32]{0:T(128)S(1)}, ...), condition=%wide.region_4.0_spmd.clone, body=%wide.region_1.0_spmd.clone.sunk | while | flops 22880256 | bytes 33503556 | solution.py:88
  44.5 0.1 broadcast_subtract_fusion.2
  44.6 0.6 subtract_bitcast_fusion.2
  45.2 0.5 constant_dynamic-update-slice_fusion.25
  45.8 0.1 constant_dynamic-update-slice_fusion.27
  46.0 0.1 constant_dynamic-update-slice_fusion.33
  46.1 0.1 constant_dynamic-update-slice_fusion.31
  46.2 0.1 constant_dynamic-update-slice_fusion.29
  46.2 0.1 constant_dynamic-update-slice_fusion.28
  46.3 0.2 subtract_dynamic-update-slice_fusion.2
  46.6 0.0 copy-start
  46.6 1.3 %copy-done = f32[32,256,64]{1,2,0:T(8,128)} copy-done((f32[32,256,64]{1,2,0:T(8,128)}, f32[32,256,64]{1,2,0:T(8,128)S(1)}, u32[]{:S(2)}) %copy-start) | copy-done | bytes 2097176 | tf_op jit(solution)/shard_map/while
  47.9 0.1 copy.38
  48.1 0.2 fusion.24
  48.3 0.1 broadcast_multiply_fusion.3
  48.4 3.7 %add_reduce_fusion.2 = (f32[32,64]{1,0:T(8,128)S(1)}, f32[32,64]{1,0:T(8,128)S(1)}) fusion(f32[32,256,64]{1,2,0:T(8,128)S(1)} %get-tuple-element.339, f32[32,256,64]{1,2,0:T(8,128)} %copy-done, f32[32,256]{1,0:T(8,128)S(1)} %get-tuple-element.343, f32[32,256]{1,0:T(8,128)S(1)} %get-tuple-element.344, f32[32,256]{1,0:T(8,128)S(1)} %get-tuple-element.347, ...), kind=kLoop, calls=%fused_computation.1.clone.1 | loop fusion | flops 14675968 | bytes 4735104 | tf_op jit(solution)/shard_map/while/body/eval_jaxpr/reduce_sum | solution.py:48
  52.2 0.1 broadcast_subtract_fusion.2
  52.4 0.6 subtract_bitcast_fusion.2
  52.9 0.5 constant_dynamic-update-slice_fusion.25
  53.6 0.1 constant_dynamic-update-slice_fusion.27
  53.7 0.1 constant_dynamic-update-slice_fusion.33
  53.8 0.1 constant_dynamic-update-slice_fusion.31
  53.9 0.1 constant_dynamic-update-slice_fusion.29
  54.0 0.1 constant_dynamic-update-slice_fusion.28
  54.1 0.2 subtract_dynamic-update-slice_fusion.2
  54.3 0.0 copy-start
  54.3 1.3 %copy-done = f32[32,256,64]{1,2,0:T(8,128)} copy-done((f32[32,256,64]{1,2,0:T(8,128)}, f32[32,256,64]{1,2,0:T(8,128)S(1)}, u32[]{:S(2)}) %copy-start) | copy-done | bytes 2097176 | tf_op jit(solution)/shard_map/while
  55.7 0.1 copy.38
  55.8 0.2 fusion.24
  56.0 0.1 broadcast_multiply_fusion.3
  56.2 3.7 %add_reduce_fusion.2 = (f32[32,64]{1,0:T(8,128)S(1)}, f32[32,64]{1,0:T(8,128)S(1)}) fusion(f32[32,256,64]{1,2,0:T(8,128)S(1)} %get-tuple-element.339, f32[32,256,64]{1,2,0:T(8,128)} %copy-done, f32[32,256]{1,0:T(8,128)S(1)} %get-tuple-element.343, f32[32,256]{1,0:T(8,128)S(1)} %get-tuple-element.344, f32[32,256]{1,0:T(8,128)S(1)} %get-tuple-element.347, ...), kind=kLoop, calls=%fused_computation.1.clone.1 | loop fusion | flops 14675968 | bytes 4735104 | tf_op jit(solution)/shard_map/while/body/eval_jaxpr/reduce_sum | solution.py:48
  60.0 0.0 copy-start.2
  60.0 0.1 fusion.16
  60.1 1.6 %collective-permute-start = (f32[64]{0:T(128)S(1)}, f32[64]{0:T(128)S(1)}, u32[]{:S(2)}, u32[]{:S(2)}) collective-permute-start(f32[64]{0:T(128)S(1)} %fusion.16), channel_id=1, source_target_pairs={{0,1},{1,0},{2,3},{3,2},{4,5},{5,4},{6,7},{7,6},{8,9},{9,8},{10,11... | collective-permute-start | bytes 776 | tf_op jit(solution)/shard_map/ppermute | solution.py:92
  61.6 2.0 %collective-permute-done = f32[64]{0:T(128)S(1)} collective-permute-done((f32[64]{0:T(128)S(1)}, f32[64]{0:T(128)S(1)}, u32[]{:S(2)}, u32[]{:S(2)}) %collective-permute-start) | collective-permute-done | bytes 288 | tf_op jit(solution)/shard_map/ppermute | solution.py:92
  63.7 0.5 add_log_fusion
  64.2 0.0 copy-done.2
  (32 shorter events, 0.5 us)
Async XLA Ops:
  0.6 43.9 %copy-start.3 = (f32[3,512]{1,0:T(4,128)S(1)}, f32[3,512]{1,0:T(4,128)}, u32[]{:S(2)}) copy-start(f32[3,512]{1,0:T(4,128)} %param.12) | copy-start | bytes 18436
  0.6 43.8 %copy-start.1 = (f32[3,64]{1,0:T(4,128)S(1)}, f32[3,64]{1,0:T(4,128)}, u32[]{:S(2)}) copy-start(f32[3,64]{1,0:T(4,128)} %param.13) | copy-start | bytes 2308
  25.9 18.6 %all-to-all-start.1 = ((f32[16,32,256]{2,1,0:T(8,128)}), f32[16,32,256]{2,1,0:T(8,128)S(1)}, u32[]{:S(2)}, u32[]{:S(2)}) async-start(f32[16,32,256]{2,1,0:T(8,128)} %broadcast_in_dim.41), calls=%async_computation.1 | async-start | bytes 1048576 | tf_op jit(solution)/shard_map/all_to_all | solution.py:75
  46.6 1.3 %copy-start = (f32[32,256,64]{1,2,0:T(8,128)}, f32[32,256,64]{1,2,0:T(8,128)S(1)}, u32[]{:S(2)}) copy-start(f32[32,256,64]{1,2,0:T(8,128)S(1)} %get-tuple-element.340) | copy-start | bytes 6291460 | tf_op jit(solution)/shard_map/while
  54.3 1.3 %copy-start = (f32[32,256,64]{1,2,0:T(8,128)}, f32[32,256,64]{1,2,0:T(8,128)S(1)}, u32[]{:S(2)}) copy-start(f32[32,256,64]{1,2,0:T(8,128)S(1)} %get-tuple-element.340) | copy-start | bytes 6291460 | tf_op jit(solution)/shard_map/while
  60.0 4.2 %copy-start.2 = (f32[32,2,64]{2,1,0:T(2,128)}, f32[32,2,64]{2,1,0:T(2,128)S(1)}, u32[]{:S(2)}) copy-start(f32[32,2,64]{2,1,0:T(2,128)S(1)} %copy_multiply_fusion) | copy-start | bytes 49156
  60.1 3.6 %collective-permute-start = (f32[64]{0:T(128)S(1)}, f32[64]{0:T(128)S(1)}, u32[]{:S(2)}, u32[]{:S(2)}) collective-permute-start(f32[64]{0:T(128)S(1)} %fusion.16), channel_id=1, source_target_pairs={{0,1},{1,0},{2,3},{3,2},{4,5},{5,4},{6,7},{7,6},{8,9},{9,8},{10,11... | collective-permute-start | bytes 776 | tf_op jit(solution)/shard_map/ppermute | solution.py:92
where the time goes:
time: 64.6 us; the launch traced here: 64.2 us
  blocking collectives  21.6 us (33%)
  waiting for transfers between devices  16.5 us (26%)
  other arithmetic  13.5 us (21%)
  starting transfers between devices  5.68 us (9%)
  local copies, waits for them, and re-layouts  4.35 us (7%)
  matrix products  1.36 us (2%)
  between operations  0.71 us (1%)
    all_to_all x1, blocking collectives, shards(): lax.all_to_all(local_source.reshape(groups, panels_dev, columns), 'obs',...  21.6 us
    all_to_all x1, waiting for transfers between devices, shards(): lax.all_to_all(jnp.broadcast_to(own_source[None], (groups, panels_dev, co...  14.4 us
    reduce_sum x2, other arithmetic, kernel_block(): real_part = jnp.sum(weight_real * amp_real + weight_imag * amp_imag, axis=1)  7.48 us
    all_to_all x1, starting transfers between devices, shards(): lax.all_to_all(jnp.broadcast_to(own_source[None], (groups, panels_dev, co...  4.1 us
    while x18, local copies, waits for them, and re-layouts  2.8 us
    ppermute x1, waiting for transfers between devices, shards(): band_total = energy + lax.ppermute(energy, 'freq', [(0, 1), (1, 0)])  2.02 us
    while x12, other arithmetic  1.71 us
    ppermute x1, starting transfers between devices, shards(): band_total = energy + lax.ppermute(energy, 'freq', [(0, 1), (1, 0)])  1.58 us
  transfers between devices with their start and end apart: 2, of which 2 were waited for; matrix products, arithmetic and copies ran while one was open for 0% of the time, Pallas kernels for 0%

commit v1 on v0

--- a/solution.py
+++ b/solution.py
@@ -3,9 +3,24 @@
 import jax.numpy as jnp
 from jax import lax
 from jax.sharding import PartitionSpec as P
+from jax.lax import axis_index, ppermute, psum
 
 wave_step = 0.1
 reference_radius = 10.0
+
+
+def manage_regions(array_here, pos_dim, point):
+    h_now = array_here.shape
+    carry_out = array_here.reshape(
+        *h_now[:pos_dim], point, h_now[pos_dim] // point, *h_now[pos_dim + 1 :]
+    )
+    return jnp.moveaxis(carry_out, pos_dim, 0)
+
+
+def prepare_regions(here_x, d0):
+    here_x = jnp.moveaxis(here_x, 0, d0)
+    e_now = here_x.shape
+    return here_x.reshape(*e_now[:d0], e_now[d0] * e_now[d0 + 1], *e_now[d0 + 2 :])
 
 
 def phase_powers(distance, wave_numbers):
@@ -72,8 +87,22 @@
         local_source.reshape(groups, panels_dev, columns), "obs", 0, 0, tiled=True
     )
     own_source = jnp.sum(arrived, axis=0)
-    portion = lax.all_to_all(
-        jnp.broadcast_to(own_source[None], (groups, panels_dev, columns)), "obs", 0, 0, tiled=True
+
+    def touch_goods(target, comm_axis, tile_in, raw):
+        upper = psum(1, axis_name=comm_axis)
+        new, current_value = (upper, axis_index(comm_axis))
+        field_out = manage_regions(target, tile_in, new)
+        views = [field_out[current_value]]
+        for idx in tuple(range(1, new)):
+            v1 = field_out[current_value ^ idx]
+            m_next = ppermute(v1, axis_name=comm_axis, perm=[(u, u ^ idx) for u in range(new)])
+            views.append(m_next)
+        value_now = jnp.stack(views, axis=0)
+        field_out = value_now[current_value ^ jnp.arange(new)]
+        return prepare_regions(field_out, raw)
+
+    portion = touch_goods(
+        jnp.broadcast_to(own_source[None], (groups, panels_dev, columns)), "obs", 0, 0
     ).reshape(panel_total, columns)
     rows_count = portion.shape[0]
     tile_rows = math.gcd(rows_count, 256)

time: 64.6 us -> 72 us (1.11)
  starting transfers between devices: 5.68 us -> 29.4 us
  blocking collectives: 21.6 us -> 0 us
  waiting for transfers between devices: 16.5 us -> 21.1 us
  matrix products: 1.36 us -> 2.19 us
    all_to_all x1 -> x0, blocking collectives: 21.6 us -> none  [shards(): lax.all_to_all(local_source.reshape(groups, panels_dev, columns), 'obs',...]
    ppermute x0 -> x15, starting transfers between devices: none -> 20.5 us  [touch_goods(): ppermute(v1, axis_name=comm_axis, perm=[(u, u ^ idx) for u in range(new)])]
    ppermute x0 -> x15, waiting for transfers between devices: none -> 4.68 us  [touch_goods(): ppermute(v1, axis_name=comm_axis, perm=[(u, u ^ idx) for u in range(new)])]
    all_to_all x1, starting transfers between devices: 4.1 us -> 7.36 us  [shards(): lax.all_to_all(local_source.reshape(groups, panels_dev, columns), 'obs',...]
    broadcast_in_dim x1 -> x0, local copies, waits for them, and re-layouts: 0.84 us -> none  [shards(): jnp.broadcast_to(own_source[None], (groups, panels_dev, columns))]
    dot_general x1, matrix products: 1.36 us -> 2.19 us  [shards(): jnp.dot(selector, weighted, preferred_element_type=jnp.float32)]
  transfers between devices with their start and end apart: 2 -> 17, of which waited for: 2 -> 4; matrix products, arithmetic and copies ran while one was open for 0% -> 0% of each run, Pallas kernels for 0% -> 0%
where the time goes in v1:
time: 72 us; the launch traced here: 71.7 us
  starting transfers between devices  29.4 us (41%)
  waiting for transfers between devices  21.1 us (29%)
  other arithmetic  13.6 us (19%)
  local copies, waits for them, and re-layouts  4.16 us (6%)
  matrix products  2.19 us (3%)
  between operations  0.79 us (1%)
    ppermute x15, starting transfers between devices, touch_goods(): ppermute(v1, axis_name=comm_axis, perm=[(u, u ^ idx) for u in range(new)])  20.5 us
    all_to_all x1, waiting for transfers between devices, shards(): lax.all_to_all(local_source.reshape(groups, panels_dev, columns), 'obs',...  14.4 us
    reduce_sum x2, other arithmetic, kernel_block(): real_part = jnp.sum(weight_real * amp_real + weight_imag * amp_imag, axis=1)  7.48 us
    all_to_all x1, starting transfers between devices, shards(): lax.all_to_all(local_source.reshape(groups, panels_dev, columns), 'obs',...  7.36 us
    ppermute x15, waiting for transfers between devices, touch_goods(): ppermute(v1, axis_name=comm_axis, perm=[(u, u ^ idx) for u in range(new)])  4.68 us
    while x18, local copies, waits for them, and re-layouts  2.8 us
    dot_general x1, matrix products, shards(): jnp.dot(selector, weighted, preferred_element_type=jnp.float32)  2.19 us
    ppermute x1, waiting for transfers between devices, shards(): band_total = energy + lax.ppermute(energy, 'freq', [(0, 1), (1, 0)])  2.02 us
  transfers between devices with their start and end apart: 17, of which 4 were waited for; matrix products, arithmetic and copies ran while one was open for 0% of the time, Pallas kernels for 0%

profile of v1, /device:TPU:0, one launch (start us, length us, event | category | flops | bytes accessed | tf_op | source)
XLA Modules:
  0.0 71.7 jit_solution(6381374551735919344)
XLA Ops:
  0.6 0.7 broadcast_multiply_fusion.1
  1.3 0.7 add.304
  2.0 2.2 %fusion.12 = f32[512,256]{1,0:T(8,128)} fusion(s32[512]{0:T(512)S(1)} %add.304, bf16[512,256]{1,0:T(8,128)(2,1)} %param.8, f32[512]{0:T(512)} %param.9), kind=kOutput, calls=%fused_computation.84 | convolution fusion | flops 134873088 | bytes 790528 | tf_op jit(solution)/shard_map/dot_general | solution.py:80
  4.2 7.4 %all-to-all-start = ((f32[16,32,256]{2,1,0:T(8,128)}), f32[16,32,256]{2,1,0:T(8,128)S(1)}, u32[]{:S(2)}, u32[]{:S(2)}) async-start(f32[16,32,256]{2,1,0:T(8,128)} %bitcast.1), calls=%async_computation | async-start | bytes 1048576 | tf_op jit(solution)/shard_map/all_to_all | solution.py:86
  11.6 14.4 %all-to-all-done = f32[16,32,256]{2,1,0:T(8,128)S(1)} async-done(((f32[16,32,256]{2,1,0:T(8,128)}), f32[16,32,256]{2,1,0:T(8,128)S(1)}, u32[]{:S(2)}, u32[]{:S(2)}) %all-to-all-start) | async-done | bytes 524320 | tf_op jit(solution)/shard_map/all_to_all | solution.py:86
  26.1 0.1 collective-permute-start
  26.2 1.1 %collective-permute-start.1 = (f32[1,32,256]{2,1,0:T(8,128)S(1)}, f32[1,32,256]{2,1,0:T(8,128)S(1)}, u32[]{:S(2)}, u32[]{:S(2)}) collective-permute-start(f32[1,32,256]{2,1,0:T(8,128)S(1)} %bitcast.146), channel_id=1, source_target_pairs={{0,4},{2,6},{4,0},{6,2},{8,12},{10,14},{12,8},{14,10},{16,20},{18,... | collective-permute-start | bytes 98312 | tf_op jit(solution)/shard_map/ppermute | solution.py:98
  27.3 0.7 collective-permute-start.2
  28.0 1.3 %collective-permute-start.3 = (f32[1,32,256]{2,1,0:T(8,128)S(1)}, f32[1,32,256]{2,1,0:T(8,128)S(1)}, u32[]{:S(2)}, u32[]{:S(2)}) collective-permute-start(f32[1,32,256]{2,1,0:T(8,128)S(1)} %bitcast.148), channel_id=1, source_target_pairs={{0,8},{2,10},{4,12},{6,14},{8,0},{10,2},{12,4},{14,6},{16,24},{18,... | collective-permute-start | bytes 98312 | tf_op jit(solution)/shard_map/ppermute | solution.py:98
  29.3 0.4 collective-permute-start.4
  29.7 0.0 collective-permute-done
  29.7 2.0 %collective-permute-start.5 = (f32[1,32,256]{2,1,0:T(8,128)S(1)}, f32[1,32,256]{2,1,0:T(8,128)S(1)}, u32[]{:S(2)}, u32[]{:S(2)}) collective-permute-start(f32[1,32,256]{2,1,0:T(8,128)S(1)} %bitcast.150), channel_id=1, source_target_pairs={{0,12},{2,14},{4,8},{6,10},{8,4},{10,6},{12,0},{14,2},{16,28},{18,... | collective-permute-start | bytes 98312 | tf_op jit(solution)/shard_map/ppermute | solution.py:98
  31.7 0.0 collective-permute-done.1
  31.7 0.7 collective-permute-start.6
  32.4 2.3 %collective-permute-start.7 = (f32[1,32,256]{2,1,0:T(8,128)S(1)}, f32[1,32,256]{2,1,0:T(8,128)S(1)}, u32[]{:S(2)}, u32[]{:S(2)}) collective-permute-start(f32[1,32,256]{2,1,0:T(8,128)S(1)} %bitcast.152), channel_id=1, source_target_pairs={{0,16},{2,18},{4,20},{6,22},{8,24},{10,26},{12,28},{14,30},{16,0},... | collective-permute-start | bytes 98312 | tf_op jit(solution)/shard_map/ppermute | solution.py:98
  34.7 0.0 collective-permute-done.3
  34.7 0.3 collective-permute-start.8
  35.0 0.0 collective-permute-done.4
  35.0 1.8 %collective-permute-start.9 = (f32[1,32,256]{2,1,0:T(8,128)S(1)}, f32[1,32,256]{2,1,0:T(8,128)S(1)}, u32[]{:S(2)}, u32[]{:S(2)}) collective-permute-start(f32[1,32,256]{2,1,0:T(8,128)S(1)} %bitcast.154), channel_id=1, source_target_pairs={{0,20},{2,22},{4,16},{6,18},{8,28},{10,30},{12,24},{14,26},{16,4},... | collective-permute-start | bytes 98312 | tf_op jit(solution)/shard_map/ppermute | solution.py:98
  36.8 0.0 collective-permute-done.5
  36.8 1.8 %collective-permute-start.10 = (f32[1,32,256]{2,1,0:T(8,128)S(1)}, f32[1,32,256]{2,1,0:T(8,128)S(1)}, u32[]{:S(2)}, u32[]{:S(2)}) collective-permute-start(f32[1,32,256]{2,1,0:T(8,128)S(1)} %bitcast.155), channel_id=1, source_target_pairs={{0,22},{2,20},{4,18},{6,16},{8,30},{10,28},{12,26},{14,24},{16,6},... | collective-permute-start | bytes 98312 | tf_op jit(solution)/shard_map/ppermute | solution.py:98
  38.6 1.7 %collective-permute-start.11 = (f32[1,32,256]{2,1,0:T(8,128)S(1)}, f32[1,32,256]{2,1,0:T(8,128)S(1)}, u32[]{:S(2)}, u32[]{:S(2)}) collective-permute-start(f32[1,32,256]{2,1,0:T(8,128)S(1)} %bitcast.156), channel_id=1, source_target_pairs={{0,24},{2,26},{4,28},{6,30},{8,16},{10,18},{12,20},{14,22},{16,8},... | collective-permute-start | bytes 98312 | tf_op jit(solution)/shard_map/ppermute | solution.py:98
  40.4 0.0 collective-permute-done.7
  40.4 1.8 %collective-permute-start.12 = (f32[1,32,256]{2,1,0:T(8,128)S(1)}, f32[1,32,256]{2,1,0:T(8,128)S(1)}, u32[]{:S(2)}, u32[]{:S(2)}) collective-permute-start(f32[1,32,256]{2,1,0:T(8,128)S(1)} %bitcast.157), channel_id=1, source_target_pairs={{0,26},{2,24},{4,30},{6,28},{8,18},{10,16},{12,22},{14,20},{16,10}... | collective-permute-start | bytes 98312 | tf_op jit(solution)/shard_map/ppermute | solution.py:98
  42.2 2.9 %collective-permute-start.13 = (f32[1,32,256]{2,1,0:T(8,128)S(1)}, f32[1,32,256]{2,1,0:T(8,128)S(1)}, u32[]{:S(2)}, u32[]{:S(2)}) collective-permute-start(f32[1,32,256]{2,1,0:T(8,128)S(1)} %bitcast.158), channel_id=1, source_target_pairs={{0,28},{2,30},{4,24},{6,26},{8,20},{10,22},{12,16},{14,18},{16,12}... | collective-permute-start | bytes 98312 | tf_op jit(solution)/shard_map/ppermute | solution.py:98
  45.1 1.6 %collective-permute-start.14 = (f32[1,32,256]{2,1,0:T(8,128)S(1)}, f32[1,32,256]{2,1,0:T(8,128)S(1)}, u32[]{:S(2)}, u32[]{:S(2)}) collective-permute-start(f32[1,32,256]{2,1,0:T(8,128)S(1)} %bitcast.159), channel_id=1, source_target_pairs={{0,30},{2,28},{4,26},{6,24},{8,22},{10,20},{12,18},{14,16},{16,14}... | collective-permute-start | bytes 98312 | tf_op jit(solution)/shard_map/ppermute | solution.py:98
  46.7 0.0 collective-permute-done.12
  46.7 2.1 %collective-permute-done.13 = f32[1,32,256]{2,1,0:T(8,128)S(1)} collective-permute-done((f32[1,32,256]{2,1,0:T(8,128)S(1)}, f32[1,32,256]{2,1,0:T(8,128)S(1)}, u32[]{:S(2)}, u32[]{:S(2)}) %collective-permute-start.13) | collective-permute-done | bytes 32800 | tf_op jit(solution)/shard_map/ppermute | solution.py:98
  48.8 2.6 %collective-permute-done.14 = f32[1,32,256]{2,1,0:T(8,128)S(1)} collective-permute-done((f32[1,32,256]{2,1,0:T(8,128)S(1)}, f32[1,32,256]{2,1,0:T(8,128)S(1)}, u32[]{:S(2)}, u32[]{:S(2)}) %collective-permute-start.14) | collective-permute-done | bytes 32800 | tf_op jit(solution)/shard_map/ppermute | solution.py:98
  51.4 0.6 gather_fusion
  52.0 15.5 %while.14 = (s32[]{:T(128)}, f32[32,2,64]{2,0,1:T(8,128)S(1)}, f32[32]{0:T(128)S(1)}, f32[3,64]{1,0:T(4,128)S(1)}, f32[3,512]{1,0:T(4,128)S(1)}, /*index=5*/f32[...) while((s32[]{:T(128)}, f32[32,2,64]{2,0,1:T(8,128)S(1)}, f32[32]{0:T(128)S(1)}, ...), condition=%wide.region_4.0_spmd.clone, body=%wide.region_1.0_spmd.clone.sunk | while | flops 22880256 | bytes 33503556 | solution.py:117
  52.0 0.1 broadcast_subtract_fusion.2
  52.1 0.6 subtract_bitcast_fusion.2
  52.7 0.5 constant_dynamic-update-slice_fusion.41
  53.4 0.1 constant_dynamic-update-slice_fusion.43
  53.5 0.1 constant_dynamic-update-slice_fusion.49
  53.6 0.1 constant_dynamic-update-slice_fusion.47
  53.7 0.1 constant_dynamic-update-slice_fusion.45
  53.8 0.1 constant_dynamic-update-slice_fusion.44
  53.9 0.2 subtract_dynamic-update-slice_fusion.2
  54.1 1.3 %copy-done = f32[32,256,64]{1,2,0:T(8,128)} copy-done((f32[32,256,64]{1,2,0:T(8,128)}, f32[32,256,64]{1,2,0:T(8,128)S(1)}, u32[]{:S(2)}) %copy-start) | copy-done | bytes 2097176 | tf_op jit(solution)/shard_map/while
  55.4 0.1 copy.68
  55.6 0.2 fusion.25
  55.8 0.1 broadcast_multiply_fusion.3
  56.0 3.7 %add_reduce_fusion.2 = (f32[32,64]{1,0:T(8,128)S(1)}, f32[32,64]{1,0:T(8,128)S(1)}) fusion(f32[32,256,64]{1,2,0:T(8,128)S(1)} %get-tuple-element.339, f32[32,256,64]{1,2,0:T(8,128)} %copy-done, f32[32,256]{1,0:T(8,128)S(1)} %get-tuple-element.343, f32[32,256]{1,0:T(8,128)S(1)} %get-tuple-element.344, f32[32,256]{1,0:T(8,128)S(1)} %get-tuple-element.347, ...), kind=kLoop, calls=%fused_computation.2.clone.1 | loop fusion | flops 14675968 | bytes 4735104 | tf_op jit(solution)/shard_map/while/body/eval_jaxpr/reduce_sum | solution.py:63
  59.8 0.1 broadcast_subtract_fusion.2
  59.9 0.6 subtract_bitcast_fusion.2
  60.5 0.5 constant_dynamic-update-slice_fusion.41
  61.1 0.1 constant_dynamic-update-slice_fusion.43
  61.2 0.1 constant_dynamic-update-slice_fusion.49
  61.3 0.1 constant_dynamic-update-slice_fusion.47
  61.4 0.1 constant_dynamic-update-slice_fusion.45
  61.5 0.1 constant_dynamic-update-slice_fusion.44
  61.6 0.2 subtract_dynamic-update-slice_fusion.2
  61.8 1.3 %copy-done = f32[32,256,64]{1,2,0:T(8,128)} copy-done((f32[32,256,64]{1,2,0:T(8,128)}, f32[32,256,64]{1,2,0:T(8,128)S(1)}, u32[]{:S(2)}) %copy-start) | copy-done | bytes 2097176 | tf_op jit(solution)/shard_map/while
  63.2 0.1 copy.68
  63.3 0.2 fusion.25
  63.6 0.1 broadcast_multiply_fusion.3
  63.7 3.7 %add_reduce_fusion.2 = (f32[32,64]{1,0:T(8,128)S(1)}, f32[32,64]{1,0:T(8,128)S(1)}) fusion(f32[32,256,64]{1,2,0:T(8,128)S(1)} %get-tuple-element.339, f32[32,256,64]{1,2,0:T(8,128)} %copy-done, f32[32,256]{1,0:T(8,128)S(1)} %get-tuple-element.343, f32[32,256]{1,0:T(8,128)S(1)} %get-tuple-element.344, f32[32,256]{1,0:T(8,128)S(1)} %get-tuple-element.347, ...), kind=kLoop, calls=%fused_computation.2.clone.1 | loop fusion | flops 14675968 | bytes 4735104 | tf_op jit(solution)/shard_map/while/body/eval_jaxpr/reduce_sum | solution.py:63
  67.5 0.0 copy-start.2
  67.5 0.1 fusion.16
  67.6 1.6 %collective-permute-start.15 = (f32[64]{0:T(128)S(1)}, f32[64]{0:T(128)S(1)}, u32[]{:S(2)}, u32[]{:S(2)}) collective-permute-start(f32[64]{0:T(128)S(1)} %fusion.16), channel_id=1, source_target_pairs={{0,1},{1,0},{2,3},{3,2},{4,5},{5,4},{6,7},{7,6},{8,9},{9,8},{10,11... | collective-permute-start | bytes 776 | tf_op jit(solution)/shard_map/ppermute | solution.py:121
  69.2 2.0 %collective-permute-done.15 = f32[64]{0:T(128)S(1)} collective-permute-done((f32[64]{0:T(128)S(1)}, f32[64]{0:T(128)S(1)}, u32[]{:S(2)}, u32[]{:S(2)}) %collective-permute-start.15) | collective-permute-done | bytes 288 | tf_op jit(solution)/shard_map/ppermute | solution.py:121
  71.2 0.5 add_log_fusion
  (63 shorter events, 0.6 us)
Async XLA Ops:
  2.0 50.0 %copy-start.1 = (f32[3,64]{1,0:T(4,128)S(1)}, f32[3,64]{1,0:T(4,128)}, u32[]{:S(2)}) copy-start(f32[3,64]{1,0:T(4,128)} %param.13) | copy-start | bytes 2308
  2.0 50.0 %copy-start.3 = (f32[3,512]{1,0:T(4,128)S(1)}, f32[3,512]{1,0:T(4,128)}, u32[]{:S(2)}) copy-start(f32[3,512]{1,0:T(4,128)} %param.12) | copy-start | bytes 18436
  4.2 21.8 %all-to-all-start = ((f32[16,32,256]{2,1,0:T(8,128)}), f32[16,32,256]{2,1,0:T(8,128)S(1)}, u32[]{:S(2)}, u32[]{:S(2)}) async-start(f32[16,32,256]{2,1,0:T(8,128)} %bitcast.1), calls=%async_computation | async-start | bytes 1048576 | tf_op jit(solution)/shard_map/all_to_all | solution.py:86
  26.1 3.7 %collective-permute-start = (f32[1,32,256]{2,1,0:T(8,128)S(1)}, f32[1,32,256]{2,1,0:T(8,128)S(1)}, u32[]{:S(2)}, u32[]{:S(2)}) collective-permute-start(f32[1,32,256]{2,1,0:T(8,128)S(1)} %bitcast.145), channel_id=1, source_target_pairs={{0,2},{2,0},{4,6},{6,4},{8,10},{10,8},{12,14},{14,12},{16,18},{18,... | collective-permute-start | bytes 98312 | tf_op jit(solution)/shard_map/ppermute | solution.py:98
  26.2 5.6 %collective-permute-start.1 = (f32[1,32,256]{2,1,0:T(8,128)S(1)}, f32[1,32,256]{2,1,0:T(8,128)S(1)}, u32[]{:S(2)}, u32[]{:S(2)}) collective-permute-start(f32[1,32,256]{2,1,0:T(8,128)S(1)} %bitcast.146), channel_id=1, source_target_pairs={{0,4},{2,6},{4,0},{6,2},{8,12},{10,14},{12,8},{14,10},{16,20},{18,... | collective-permute-start | bytes 98312 | tf_op jit(solution)/shard_map/ppermute | solution.py:98
  27.3 5.1 %collective-permute-start.2 = (f32[1,32,256]{2,1,0:T(8,128)S(1)}, f32[1,32,256]{2,1,0:T(8,128)S(1)}, u32[]{:S(2)}, u32[]{:S(2)}) collective-permute-start(f32[1,32,256]{2,1,0:T(8,128)S(1)} %bitcast.147), channel_id=1, source_target_pairs={{0,6},{2,4},{4,2},{6,0},{8,14},{10,12},{12,10},{14,8},{16,22},{18,... | collective-permute-start | bytes 98312 | tf_op jit(solution)/shard_map/ppermute | solution.py:98
  28.0 6.7 %collective-permute-start.3 = (f32[1,32,256]{2,1,0:T(8,128)S(1)}, f32[1,32,256]{2,1,0:T(8,128)S(1)}, u32[]{:S(2)}, u32[]{:S(2)}) collective-permute-start(f32[1,32,256]{2,1,0:T(8,128)S(1)} %bitcast.148), channel_id=1, source_target_pairs={{0,8},{2,10},{4,12},{6,14},{8,0},{10,2},{12,4},{14,6},{16,24},{18,... | collective-permute-start | bytes 98312 | tf_op jit(solution)/shard_map/ppermute | solution.py:98
  29.3 5.7 %collective-permute-start.4 = (f32[1,32,256]{2,1,0:T(8,128)S(1)}, f32[1,32,256]{2,1,0:T(8,128)S(1)}, u32[]{:S(2)}, u32[]{:S(2)}) collective-permute-start(f32[1,32,256]{2,1,0:T(8,128)S(1)} %bitcast.149), channel_id=1, source_target_pairs={{0,10},{2,8},{4,14},{6,12},{8,2},{10,0},{12,6},{14,4},{16,26},{18,... | collective-permute-start | bytes 98312 | tf_op jit(solution)/shard_map/ppermute | solution.py:98
  29.7 7.1 %collective-permute-start.5 = (f32[1,32,256]{2,1,0:T(8,128)S(1)}, f32[1,32,256]{2,1,0:T(8,128)S(1)}, u32[]{:S(2)}, u32[]{:S(2)}) collective-permute-start(f32[1,32,256]{2,1,0:T(8,128)S(1)} %bitcast.150), channel_id=1, source_target_pairs={{0,12},{2,14},{4,8},{6,10},{8,4},{10,6},{12,0},{14,2},{16,28},{18,... | collective-permute-start | bytes 98312 | tf_op jit(solution)/shard_map/ppermute | solution.py:98
  31.7 6.9 %collective-permute-start.6 = (f32[1,32,256]{2,1,0:T(8,128)S(1)}, f32[1,32,256]{2,1,0:T(8,128)S(1)}, u32[]{:S(2)}, u32[]{:S(2)}) collective-permute-start(f32[1,32,256]{2,1,0:T(8,128)S(1)} %bitcast.151), channel_id=1, source_target_pairs={{0,14},{2,12},{4,10},{6,8},{8,6},{10,4},{12,2},{14,0},{16,30},{18,... | collective-permute-start | bytes 98312 | tf_op jit(solution)/shard_map/ppermute | solution.py:98
  32.4 8.0 %collective-permute-start.7 = (f32[1,32,256]{2,1,0:T(8,128)S(1)}, f32[1,32,256]{2,1,0:T(8,128)S(1)}, u32[]{:S(2)}, u32[]{:S(2)}) collective-permute-start(f32[1,32,256]{2,1,0:T(8,128)S(1)} %bitcast.152), channel_id=1, source_target_pairs={{0,16},{2,18},{4,20},{6,22},{8,24},{10,26},{12,28},{14,30},{16,0},... | collective-permute-start | bytes 98312 | tf_op jit(solution)/shard_map/ppermute | solution.py:98
  34.7 7.5 %collective-permute-start.8 = (f32[1,32,256]{2,1,0:T(8,128)S(1)}, f32[1,32,256]{2,1,0:T(8,128)S(1)}, u32[]{:S(2)}, u32[]{:S(2)}) collective-permute-start(f32[1,32,256]{2,1,0:T(8,128)S(1)} %bitcast.153), channel_id=1, source_target_pairs={{0,18},{2,16},{4,22},{6,20},{8,26},{10,24},{12,30},{14,28},{16,2},... | collective-permute-start | bytes 98312 | tf_op jit(solution)/shard_map/ppermute | solution.py:98
  35.0 10.1 %collective-permute-start.9 = (f32[1,32,256]{2,1,0:T(8,128)S(1)}, f32[1,32,256]{2,1,0:T(8,128)S(1)}, u32[]{:S(2)}, u32[]{:S(2)}) collective-permute-start(f32[1,32,256]{2,1,0:T(8,128)S(1)} %bitcast.154), channel_id=1, source_target_pairs={{0,20},{2,22},{4,16},{6,18},{8,28},{10,30},{12,24},{14,26},{16,4},... | collective-permute-start | bytes 98312 | tf_op jit(solution)/shard_map/ppermute | solution.py:98
  36.8 9.8 %collective-permute-start.10 = (f32[1,32,256]{2,1,0:T(8,128)S(1)}, f32[1,32,256]{2,1,0:T(8,128)S(1)}, u32[]{:S(2)}, u32[]{:S(2)}) collective-permute-start(f32[1,32,256]{2,1,0:T(8,128)S(1)} %bitcast.155), channel_id=1, source_target_pairs={{0,22},{2,20},{4,18},{6,16},{8,30},{10,28},{12,26},{14,24},{16,6},... | collective-permute-start | bytes 98312 | tf_op jit(solution)/shard_map/ppermute | solution.py:98
  38.6 8.0 %collective-permute-start.11 = (f32[1,32,256]{2,1,0:T(8,128)S(1)}, f32[1,32,256]{2,1,0:T(8,128)S(1)}, u32[]{:S(2)}, u32[]{:S(2)}) collective-permute-start(f32[1,32,256]{2,1,0:T(8,128)S(1)} %bitcast.156), channel_id=1, source_target_pairs={{0,24},{2,26},{4,28},{6,30},{8,16},{10,18},{12,20},{14,22},{16,8},... | collective-permute-start | bytes 98312 | tf_op jit(solution)/shard_map/ppermute | solution.py:98
  40.4 6.3 %collective-permute-start.12 = (f32[1,32,256]{2,1,0:T(8,128)S(1)}, f32[1,32,256]{2,1,0:T(8,128)S(1)}, u32[]{:S(2)}, u32[]{:S(2)}) collective-permute-start(f32[1,32,256]{2,1,0:T(8,128)S(1)} %bitcast.157), channel_id=1, source_target_pairs={{0,26},{2,24},{4,30},{6,28},{8,18},{10,16},{12,22},{14,20},{16,10}... | collective-permute-start | bytes 98312 | tf_op jit(solution)/shard_map/ppermute | solution.py:98
  42.2 6.6 %collective-permute-start.13 = (f32[1,32,256]{2,1,0:T(8,128)S(1)}, f32[1,32,256]{2,1,0:T(8,128)S(1)}, u32[]{:S(2)}, u32[]{:S(2)}) collective-permute-start(f32[1,32,256]{2,1,0:T(8,128)S(1)} %bitcast.158), channel_id=1, source_target_pairs={{0,28},{2,30},{4,24},{6,26},{8,20},{10,22},{12,16},{14,18},{16,12}... | collective-permute-start | bytes 98312 | tf_op jit(solution)/shard_map/ppermute | solution.py:98
  45.1 6.3 %collective-permute-start.14 = (f32[1,32,256]{2,1,0:T(8,128)S(1)}, f32[1,32,256]{2,1,0:T(8,128)S(1)}, u32[]{:S(2)}, u32[]{:S(2)}) collective-permute-start(f32[1,32,256]{2,1,0:T(8,128)S(1)} %bitcast.159), channel_id=1, source_target_pairs={{0,30},{2,28},{4,26},{6,24},{8,22},{10,20},{12,18},{14,16},{16,14}... | collective-permute-start | bytes 98312 | tf_op jit(solution)/shard_map/ppermute | solution.py:98
  54.1 1.3 %copy-start = (f32[32,256,64]{1,2,0:T(8,128)}, f32[32,256,64]{1,2,0:T(8,128)S(1)}, u32[]{:S(2)}) copy-start(f32[32,256,64]{1,2,0:T(8,128)S(1)} %get-tuple-element.340) | copy-start | bytes 6291460 | tf_op jit(solution)/shard_map/while
  61.8 1.3 %copy-start = (f32[32,256,64]{1,2,0:T(8,128)}, f32[32,256,64]{1,2,0:T(8,128)S(1)}, u32[]{:S(2)}) copy-start(f32[32,256,64]{1,2,0:T(8,128)S(1)} %get-tuple-element.340) | copy-start | bytes 6291460 | tf_op jit(solution)/shard_map/while
  67.5 4.2 %copy-start.2 = (f32[32,2,64]{2,1,0:T(2,128)}, f32[32,2,64]{2,1,0:T(2,128)S(1)}, u32[]{:S(2)}) copy-start(f32[32,2,64]{2,1,0:T(2,128)S(1)} %copy_multiply_fusion) | copy-start | bytes 49156
  67.6 3.6 %collective-permute-start.15 = (f32[64]{0:T(128)S(1)}, f32[64]{0:T(128)S(1)}, u32[]{:S(2)}, u32[]{:S(2)}) collective-permute-start(f32[64]{0:T(128)S(1)} %fusion.16), channel_id=1, source_target_pairs={{0,1},{1,0},{2,3},{3,2},{4,5},{5,4},{6,7},{7,6},{8,9},{9,8},{10,11... | collective-permute-start | bytes 776 | tf_op jit(solution)/shard_map/ppermute | solution.py:121
